TPU v7x, 256 devices: a whole 4x4x8 slice. The times are simulated.
256 devices in a mesh: seq: 64 (over x, z, core), tensor: 4 (over y).
Axes of the slice: x: 4, y: 4, z: 8, core: 2. Of those that a mesh axis runs over, the one named last changes fastest.
Arguments:
- hidden: bfloat16 [8192, 8192], P('seq'), may hold values from -6 to 6
- gain: bfloat16 [8192], replicated, may hold values from 0.5 to 1.5
- w_query: bfloat16 [8192, 4096], P('seq', 'tensor'), may hold values from -0.0625 to 0.0625
- q_bias: bfloat16 [4096], P('tensor'), may hold values from -3 to 3
- w_keyval: bfloat16 [8192, 2, 512], P('seq', None, 'tensor'), may hold values from -0.125 to 0.125
- kv_bias: bfloat16 [2, 512], P(None, 'tensor'), may hold values from -3 to 3
- prefix_keys: bfloat16 [2, 4096, 4, 128], P(None, 'seq', 'tensor'), may hold values from -128 to 128, as said below
- prefix_values: bfloat16 [2, 4096, 4, 128], P(None, 'seq', 'tensor'), may hold values from -6 to 6
- lengths: int32 [32], replicated, may hold values from 1 to 384, 8192 in all
- assignment: int32 [32], replicated, may hold values from 0 to 1
Outputs:
- attention: bfloat16 [8192, 4096], P('seq', 'tensor')
- suffix_keys: bfloat16 [8192, 4, 128], P('seq', 'tensor')
- suffix_values: bfloat16 [8192, 4, 128], P('seq', 'tensor')
Inputs may be any that keep to these rules, and one draw needn't show every extreme that they name: Request r occupies the next lengths[r] rows of the token arrays, in order; the lengths sum to 8192 and the largest is 384. `assignment`: the prefix that request r continues. `prefix_keys`: cached keys, already rotated to positions 0 to 4095.
All inputs are finite; a program needn't handle non-finite values.
Results may differ from a plain program's by a relative error of at most 0.01.
The roundings to bfloat16 on the way count: a program that leaves them out, or rounds other values in their place, can miss the bound.
Values may be sent and summed in bfloat16 or wider, within the bound.
No kernel may reach another device: no remote copies, remote signals or barrier semaphores. Data moves between devices by JAX's collectives and lax.ppermute only.
A program may use at most 128 MiB of HBM per device.

v0:
```python
import math
import jax
import jax.numpy as jnp
from jax import lax
from jax.sharding import PartitionSpec as P

EPS = 1e-06
THETA = 1000000.0


def from_behind(shard, axis, by):
    size = lax.axis_size(axis)
    pairs = [(i, i + by) for i in range(size) if 0 <= i + by < size]
    return lax.ppermute(shard, axis, pairs)


def row_tables(lengths, assignment, all_rows):
    request_end = jnp.cumsum(lengths)
    request_start = request_end - lengths
    row_ids = jnp.arange(all_rows, dtype=jnp.int32)
    segment = jnp.sum((row_ids[:, None] >= request_end[None, :]).astype(jnp.int32), axis=1)
    request_ids = jnp.arange(lengths.shape[0], dtype=jnp.int32)
    onehot = (segment[:, None] == request_ids[None, :]).astype(jnp.int32)
    offset = row_ids - jnp.sum(onehot * request_start[None, :], axis=1)
    prefix = jnp.sum(onehot * assignment[None, :], axis=1)
    return (segment, offset, prefix)


def rotate(values, positions):
    head_size = values.shape[-1]
    half_dim = head_size // 2
    frequency = THETA ** (-2.0 * jnp.arange(half_dim, dtype=jnp.float32) / head_size)
    angles = positions.astype(jnp.float32)[:, None] * frequency[None, :]
    cosine = jnp.concatenate([jnp.cos(angles), jnp.cos(angles)], axis=-1)[:, None, :]
    sine_part = jnp.concatenate([jnp.sin(angles), jnp.sin(angles)], axis=-1)[:, None, :]
    turned = jnp.concatenate([-values[..., half_dim:], values[..., :half_dim]], axis=-1)
    return values * cosine + turned * sine_part


def local(
    hidden,
    gain,
    w_query,
    q_bias,
    w_keyval,
    kv_bias,
    prefix_keys,
    prefix_values,
    lengths,
    assignment,
):
    row_count = hidden.shape[0]
    seq_count = lax.axis_size("seq")
    seq_index = lax.axis_index("seq")
    all_rows = row_count * seq_count
    head_dim = prefix_keys.shape[3]
    kv_local = prefix_keys.shape[2]
    prefix_count = prefix_keys.shape[0]
    query_width = w_query.shape[1]
    heads_local = query_width // head_dim
    group_size = heads_local // kv_local
    pair_width = w_keyval.shape[1] * w_keyval.shape[2]
    key_width = pair_width // 2
    cache_length = prefix_keys.shape[1] * seq_count
    score_scale = head_dim ** (-0.5)
    first_row = seq_index * row_count
    prefix_ids = jnp.arange(prefix_count, dtype=jnp.int32)
    hidden_f = hidden.astype(jnp.float32)
    normed = (
        hidden_f
        * lax.rsqrt(jnp.mean(hidden_f * hidden_f, axis=1, keepdims=True) + EPS)
        * gain.astype(jnp.float32)
    ).astype(jnp.bfloat16)
    segment, offset, prefix = row_tables(lengths, assignment, all_rows)
    positions = offset + cache_length
    own_positions = lax.dynamic_slice_in_dim(positions, first_row, row_count)
    own_segment = lax.dynamic_slice_in_dim(segment, first_row, row_count)
    own_prefix = lax.dynamic_slice_in_dim(prefix, first_row, row_count)
    w_pairs = w_keyval.reshape(w_keyval.shape[0], pair_width)
    combined = jnp.concatenate([w_query, w_pairs], axis=1)
    summed = jnp.dot(
        normed,
        lax.all_gather(combined, "seq", axis=0, tiled=True),
        preferred_element_type=jnp.float32,
    )
    query_own = summed[:, :query_width] + q_bias.astype(jnp.float32)
    pairs_own = summed[:, query_width:] + kv_bias.reshape(pair_width).astype(jnp.float32)
    own_queries = rotate(query_own.reshape(row_count, heads_local, head_dim), own_positions).astype(
        jnp.bfloat16
    )
    own_keys = rotate(
        pairs_own[:, :key_width].reshape(row_count, kv_local, head_dim), own_positions
    ).astype(jnp.bfloat16)
    own_values = (
        pairs_own[:, key_width:].reshape(row_count, kv_local, head_dim).astype(jnp.bfloat16)
    )
    own_blocks = own_queries.reshape(row_count, kv_local, group_size, head_dim)
    allowed_own = (own_prefix[:, None] == prefix_ids[None, :])[:, None, None, :, None]
    initial = (
        jnp.full((row_count, kv_local, group_size), -jnp.inf, jnp.float32),
        jnp.zeros((row_count, kv_local, group_size), jnp.float32),
        jnp.zeros((row_count, kv_local, group_size, head_dim), jnp.float32),
    )
    keys_piece = lax.all_gather(prefix_keys, "seq", axis=1, tiled=True)
    values_piece = lax.all_gather(prefix_values, "seq", axis=1, tiled=True)
    piece_len = keys_piece.shape[1]
    step_rows = math.gcd(piece_len, 512)

    def inner(state, block_index):
        run_top, run_mass, run_acc = state
        key_block = lax.dynamic_slice_in_dim(keys_piece, block_index * step_rows, step_rows, 1)
        value_block = lax.dynamic_slice_in_dim(values_piece, block_index * step_rows, step_rows, 1)
        scores = (
            jnp.einsum(
                "bgqd,plgd->bgqpl", own_blocks, key_block, preferred_element_type=jnp.float32
            )
            * score_scale
        )
        scores = jnp.where(allowed_own, scores, -jnp.inf)
        new_top = jnp.maximum(run_top, jnp.max(scores, axis=(3, 4)))
        keep_share = jnp.exp(run_top - new_top)
        weights = jnp.exp(scores - new_top[..., None, None])
        new_mass = run_mass * keep_share + jnp.sum(weights, axis=(3, 4))
        new_acc = run_acc * keep_share[..., None] + jnp.einsum(
            "bgqpl,plgd->bgqd",
            weights.astype(jnp.bfloat16),
            value_block,
            preferred_element_type=jnp.float32,
        )
        return ((new_top, new_mass, new_acc), None)

    result, unused = lax.scan(inner, initial, jnp.arange(piece_len // step_rows, dtype=jnp.int32))
    fold_top, fold_mass, fold_acc = result
    prefix_top = fold_top.reshape(row_count, heads_local)
    prefix_mass = fold_mass.reshape(row_count, heads_local)
    prefix_acc = fold_acc.reshape(row_count, heads_local, head_dim)
    pair_rows = jnp.concatenate(
        [own_keys.reshape(row_count, key_width), own_values.reshape(row_count, key_width)], axis=1
    )
    depth = min(3, seq_count - 1)
    earlier = []
    for distance in range(depth, 0, -1):
        earlier.append(from_behind(pair_rows, "seq", distance))
    near_rows = jnp.concatenate(earlier + [pair_rows], axis=0)
    near_index = (
        first_row - depth * row_count + jnp.arange((depth + 1) * row_count, dtype=jnp.int32)
    )
    near_keys = near_rows[:, :key_width].reshape(near_rows.shape[0], kv_local, head_dim)
    near_values = near_rows[:, key_width:].reshape(near_rows.shape[0], kv_local, head_dim)
    near_segment = segment[jnp.clip(near_index, 0, all_rows - 1)]
    own_rows = first_row + jnp.arange(row_count, dtype=jnp.int32)
    visible = (
        (near_index[None, :] >= 0)
        & (near_segment[None, :] == own_segment[:, None])
        & (near_index[None, :] <= own_rows[:, None])
    )
    scores = (
        jnp.einsum("bgqd,ngd->bgqn", own_blocks, near_keys, preferred_element_type=jnp.float32)
        * score_scale
    )
    scores = jnp.where(visible[:, None, None, :], scores, -jnp.inf)
    local_top = jnp.max(scores, axis=3)
    weights = jnp.exp(scores - local_top[..., None])
    local_mass = jnp.sum(weights, axis=3).reshape(row_count, heads_local)
    local_acc = jnp.einsum(
        "bgqn,ngd->bgqd",
        weights.astype(jnp.bfloat16),
        near_values,
        preferred_element_type=jnp.float32,
    ).reshape(row_count, heads_local, head_dim)
    local_top = local_top.reshape(row_count, heads_local)
    joint_top = jnp.maximum(prefix_top, local_top)
    far_scale = jnp.exp(prefix_top - joint_top)
    near_scale = jnp.exp(local_top - joint_top)
    numerator = prefix_acc * far_scale[..., None] + local_acc * near_scale[..., None]
    denominator = prefix_mass * far_scale + local_mass * near_scale
    attention = (
        (numerator / denominator[..., None]).astype(jnp.bfloat16).reshape(row_count, query_width)
    )
    return (attention, own_keys, own_values)


def solution(mesh):
    in_specs = (
        P("seq", None),
        P(),
        P("seq", "tensor"),
        P("tensor"),
        P("seq", None, "tensor"),
        P(None, "tensor"),
        P(None, "seq", "tensor", None),
        P(None, "seq", "tensor", None),
        P(),
        P(),
    )
    out_specs = (P("seq", "tensor"), P("seq", "tensor", None), P("seq", "tensor", None))
    return jax.shard_map(local, mesh=mesh, in_specs=in_specs, out_specs=out_specs, check_vma=False)
```

profile of v0, /device:TPU:1, one launch (start us, length us, event | category | flops | bytes accessed | tf_op | source)
XLA Modules:
  0.0 376.9 jit_solution(10367872859374238164)
XLA Ops:
  7.3 1.0 copy.127
  8.2 1.7 pad_maximum_fusion
  10.0 1.4 copy.68
  12.2 0.7 copy.64
  14.8 2.1 fusion.24
  17.5 3.1 gather_fusion
  22.4 102.5 %all-gather.6.cloned.1.call-done = bf16[8192,1280]{1,0:T(8,128)(2,1)} async-done(((bf16[128,1280]{1,0:T(8,128)(2,1)}), bf16[8192,1280]{1,0:T(8,128)(2,1)}) %all-gather.6.cloned.1.call-update) | async-done | bytes 20971536 | tf_op jit(solution)/shard_map/all_gather | solution.py:83
  124.9 9.9 %fusion.27 = f32[128,1280]{1,0:T(8,128)S(1)} fusion(bf16[8192,1280]{1,0:T(8,128)(2,1)} %all-gather.6.cloned.1.call-done, bf16[128,8192]{1,0:T(8,128)(2,1)S(1)} %copy-done.1, f32[8192]{0:T(1024)S(1)} %convert_element_type.68, f32[128]{0:T(128)} %add_rsqrt_fusion), kind=kOutput, calls=%fused_computation.33 | convolution fusion | flops 2688548864 | bytes 23757312 | tf_op jit(solution)/shard_map/dot_general | solution.py:81
  135.2 3.1 collective-permute-start
  138.2 4.4 %collective-permute-start.1 = (bf16[128,256]{1,0:T(8,128)(2,1)S(1)}, bf16[128,256]{1,0:T(8,128)(2,1)}, u32[]{:S(2)}, u32[]{:S(2)}) collective-permute-start(bf16[128,256]{1,0:T(8,128)(2,1)S(1)} %pad_maximum_fusion.3), channel_id=1, source_target_pairs={{0,8},{4,12},{8,16},{12,20},{16,24},{20,28},{24,32},{28,36},{32,40... | collective-permute-start | bytes 196616 | tf_op jit(solution)/shard_map/ppermute | solution.py:14
  142.7 2.2 collective-permute-start.2
  145.8 56.8 %all-gather.8.cloned.1.call-done = bf16[2,4096,1,128]{3,0,2,1:T(2,128)(2,1)} async-done(((bf16[2,64,1,128]{3,0,2,1:T(2,128)(2,1)}), bf16[2,4096,1,128]{3,0,2,1:T(2,128)(2,1)}) %all-gather.8.cloned.1.call-update) | async-done | bytes 2097168 | tf_op jit(solution)/shard_map/all_gather | solution.py:105
  202.6 77.8 %all-gather.4.cloned.1.call-done = bf16[2,4096,1,128]{3,1,0,2:T(8,128)(2,1)} async-done(((bf16[2,64,1,128]{3,1,0,2:T(8,128)(2,1)}), bf16[2,4096,1,128]{3,1,0,2:T(8,128)(2,1)}) %all-gather.4.cloned.1.call-update) | async-done | bytes 2097168 | tf_op jit(solution)/shard_map/all_gather | solution.py:104
  280.4 84.7 %while.15 = (s32[]{:T(128)}, f32[128,1,8]{0,2,1:T(8,128)S(1)}, f32[128,1,8]{0,2,1:T(8,128)S(1)}, f32[128,1,8,128]{0,3,2,1:T(8,128)S(1)}, s32[8]{0:T(128)S(1)}, /...) while((s32[]{:T(128)}, f32[128,1,8]{0,2,1:T(8,128)S(1)}, ...), condition=%wide.region_8.9_spmd.clone, body=%wide.region_5.8_spmd.clone.sunk | while | flops 548804864 | bytes 32311012 | solution.py:132
  281.6 3.6 fusion.76
  285.2 1.1 constant_dynamic-slice_fusion.2
  286.5 3.5 fusion.79
  290.1 0.8 fusion.78
  292.2 3.6 fusion.76
  295.8 1.1 constant_dynamic-slice_fusion.2
  297.1 3.5 fusion.79
  300.6 0.8 fusion.78
  302.8 3.6 fusion.76
  306.4 1.1 constant_dynamic-slice_fusion.2
  307.7 3.5 fusion.79
  311.2 0.8 fusion.78
  313.4 3.6 fusion.76
  317.0 1.1 constant_dynamic-slice_fusion.2
  318.3 3.5 fusion.79
  321.8 0.8 fusion.78
  323.9 3.6 fusion.76
  327.6 1.1 constant_dynamic-slice_fusion.2
  328.9 3.5 fusion.79
  332.4 0.8 fusion.78
  334.5 3.6 fusion.76
  338.1 1.1 constant_dynamic-slice_fusion.2
  339.5 3.5 fusion.79
  343.0 0.8 fusion.78
  345.1 3.6 fusion.76
  348.7 1.1 constant_dynamic-slice_fusion.2
  350.1 3.5 fusion.79
  353.6 0.8 fusion.78
  355.7 3.6 fusion.76
  359.3 1.1 constant_dynamic-slice_fusion.2
  360.6 3.5 fusion.79
  364.1 0.8 fusion.78
  365.9 0.9 maximum_maximum_fusion
  369.4 1.0 fusion.37
  (134 shorter events, 15.7 us)
Async XLA Ops:
  7.2 117.8 %copy-start.1 = (bf16[128,8192]{1,0:T(8,128)(2,1)S(1)}, bf16[128,8192]{1,0:T(8,128)(2,1)}, u32[]{:S(2)}) copy-start(bf16[128,8192]{1,0:T(8,128)(2,1)} %param.12) | copy-start | bytes 6291460
  7.2 13.5 %copy-start.3 = (bf16[1024]{0:T(1024)(128)(2,1)S(1)}, bf16[1024]{0:T(1024)(128)(2,1)}, u32[]{:S(2)}) copy-start(bf16[1024]{0:T(1024)(128)(2,1)} %param.15) | copy-start | bytes 6148
  7.2 13.5 %copy-start.4 = (s32[32]{0:T(128)S(1)}, s32[32]{0:T(128)}, u32[]{:S(2)}) copy-start(s32[32]{0:T(128)} %param.21) | copy-start | bytes 388
  7.2 14.6 %copy-start.5 = (bf16[2,128]{1,0:T(2,128)(2,1)S(1)}, bf16[2,128]{1,0:T(2,128)(2,1)}, u32[]{:S(2)}) copy-start(bf16[2,128]{1,0:T(2,128)(2,1)} %param.17) | copy-start | bytes 1540
  7.2 117.7 %all-gather.6.cloned.1.call-start = ((), (), s32[]{:S(2)}) async-start(), calls=%async_computation.1 | async-start | bytes 21299200 | tf_op jit(solution)/shard_map/all_gather | solution.py:83
  10.0 192.6 %all-gather.8.cloned.1.call-start = ((), (), s32[]{:S(2)}) async-start(), calls=%async_computation.2 | async-start | bytes 2129920 | tf_op jit(solution)/shard_map/all_gather | solution.py:105
  11.5 268.9 %all-gather.4.cloned.1.call-start = ((), (), s32[]{:S(2)}) async-start(), calls=%async_computation | async-start | bytes 2129920 | tf_op jit(solution)/shard_map/all_gather | solution.py:104
  135.1 230.8 %copy-start.2 = (bf16[128,128]{1,0:T(8,128)(2,1)}, bf16[128,128]{1,0:T(8,128)(2,1)S(1)}, u32[]{:S(2)}) copy-start(bf16[128,128]{1,0:T(8,128)(2,1)S(1)} %get-tuple-element.139) | copy-start | bytes 98308
  135.2 230.7 %collective-permute-start = (bf16[128,256]{1,0:T(8,128)(2,1)S(1)}, bf16[128,256]{1,0:T(8,128)(2,1)}, u32[]{:S(2)}, u32[]{:S(2)}) collective-permute-start(bf16[128,256]{1,0:T(8,128)(2,1)S(1)} %pad_maximum_fusion.3), channel_id=1, source_target_pairs={{0,12},{4,16},{8,20},{12,24},{16,28},{20,32},{24,36},{28,40},{32,4... | collective-permute-start | bytes 196616 | tf_op jit(solution)/shard_map/ppermute | solution.py:14
  138.2 227.6 %collective-permute-start.1 = (bf16[128,256]{1,0:T(8,128)(2,1)S(1)}, bf16[128,256]{1,0:T(8,128)(2,1)}, u32[]{:S(2)}, u32[]{:S(2)}) collective-permute-start(bf16[128,256]{1,0:T(8,128)(2,1)S(1)} %pad_maximum_fusion.3), channel_id=1, source_target_pairs={{0,8},{4,12},{8,16},{12,20},{16,24},{20,28},{24,32},{28,36},{32,40... | collective-permute-start | bytes 196616 | tf_op jit(solution)/shard_map/ppermute | solution.py:14
  142.7 223.2 %collective-permute-start.2 = (bf16[128,256]{1,0:T(8,128)(2,1)S(1)}, bf16[128,256]{1,0:T(8,128)(2,1)}, u32[]{:S(2)}, u32[]{:S(2)}) collective-permute-start(bf16[128,256]{1,0:T(8,128)(2,1)S(1)} %pad_maximum_fusion.3), channel_id=1, source_target_pairs={{0,4},{4,8},{8,12},{12,16},{16,20},{20,24},{24,28},{28,32},{32,36}... | collective-permute-start | bytes 196616 | tf_op jit(solution)/shard_map/ppermute | solution.py:14
  144.9 135.4 %copy-start.6 = (s32[128]{0:T(128)S(1)}, s32[128]{0:T(128)}, u32[]{:S(2)}) copy-start(s32[128]{0:T(128)} %dynamic_slice.19) | copy-start | bytes 1540
  286.5 3.5 copy-start
  297.1 3.5 copy-start
  307.7 3.5 copy-start
  318.3 3.5 copy-start
  328.9 3.5 copy-start
  339.5 3.5 copy-start
  350.0 3.5 copy-start
  360.6 3.5 copy-start
Sparse Core Ops, SparseCore 0:
  10.8 114.1 all-gather.5
  128.3 74.2 all-gather.7
  205.4 74.8 all-gather.3
where the time goes:
time: 378 us; the launch traced here: 377 us
  waiting for transfers between devices  238 us (63%)
  matrix products  67.8 us (18%)
  local copies, waits for them, and re-layouts  24.4 us (6%)
  other arithmetic  17.2 us (5%)
  between operations  14.1 us (4%)
  starting transfers between devices  9.81 us (3%)
  loops' own time  5.83 us (2%)
    all_gather x1, waiting for transfers between devices, local(): lax.all_gather(combined, 'seq', axis=0, tiled=True)  103 us
    all_gather x1, waiting for transfers between devices, local(): keys_piece = lax.all_gather(prefix_keys, 'seq', axis=1, tiled=True)  77.8 us
    all_gather x1, waiting for transfers between devices, local(): values_piece = lax.all_gather(prefix_values, 'seq', axis=1, tiled=True)  56.8 us
    dot_general x8, matrix products, inner(): jnp.einsum('bgqd,plgd->bgqpl', own_blocks, key_block, preferred_element_t...  28.9 us
    dot_general x8, matrix products, inner(): jnp.einsum('bgqpl,plgd->bgqd', weights.astype(jnp.bfloat16), value_block,...  27.9 us
    dynamic_slice x16, local copies, waits for them, and re-layouts, inner(): lax.dynamic_slice_in_dim(values_piece, block_index * step_rows, step_rows...  10.4 us
    dot_general x1, matrix products, local(): jnp.dot(normed, lax.all_gather(combined, 'seq', axis=0, tiled=True), pref...  9.93 us
    ppermute x3, starting transfers between devices, from_behind(): return lax.ppermute(shard, axis, pairs)  9.69 us
  transfers between devices with their start and end apart: 6, of which 3 were waited for; matrix products, arithmetic and copies ran while one was open for 27% of the time, Pallas kernels for 0%

commit v1 on v0

--- a/solution.py
+++ b/solution.py
@@ -102,7 +102,9 @@
         jnp.zeros((row_count, kv_local, group_size, head_dim), jnp.float32),
     )
     keys_piece = lax.all_gather(prefix_keys, "seq", axis=1, tiled=True)
-    values_piece = lax.all_gather(prefix_values, "seq", axis=1, tiled=True)
+    values_piece = jnp.concatenate(
+        lax.all_to_all(jnp.stack([prefix_values] * lax.axis_size("seq")), "seq", 0, 0), axis=1
+    )
     piece_len = keys_piece.shape[1]
     step_rows = math.gcd(piece_len, 512)
 

time: 378 us -> 311 us (0.82)
  waiting for transfers between devices: 238 us -> 167 us
  starting transfers between devices: 9.81 us -> 23 us
  local copies, waits for them, and re-layouts: 24.4 us -> 17.2 us
    all_to_all x0 -> x1, waiting for transfers between devices: none -> 57.1 us  [local(): lax.all_to_all(jnp.stack([prefix_values] * lax.axis_size('seq')), 'seq',...]
    all_gather x1 -> x0, waiting for transfers between devices: 56.8 us -> none  [local(): values_piece = lax.all_gather(prefix_values, 'seq', axis=1, tiled=True)]
    all_gather x1, waiting for transfers between devices: 103 us -> 53.1 us  [local(): lax.all_gather(combined, 'seq', axis=0, tiled=True)]
    all_gather x1, waiting for transfers between devices: 77.8 us -> 56.3 us  [local(): keys_piece = lax.all_gather(prefix_keys, 'seq', axis=1, tiled=True)]
    all_to_all x0 -> x1, starting transfers between devices: none -> 13.3 us  [local(): lax.all_to_all(jnp.stack([prefix_values] * lax.axis_size('seq')), 'seq',...]
    dynamic_slice x16 -> x0, local copies, waits for them, and re-layouts: 10.4 us -> none  [inner(): lax.dynamic_slice_in_dim(values_piece, block_index * step_rows, step_rows...]
  transfers between devices with their start and end apart: 6 -> 6, of which waited for: 3 -> 3; matrix products, arithmetic and copies ran while one was open for 27% -> 30% of each run, Pallas kernels for 0% -> 0%
where the time goes in v1:
time: 311 us; the launch traced here: 310 us
  waiting for transfers between devices  167 us (54%)
  matrix products  68.6 us (22%)
  starting transfers between devices  23 us (7%)
  local copies, waits for them, and re-layouts  17.2 us (6%)
  between operations  14.4 us (5%)
  other arithmetic  13.6 us (4%)
  loops' own time  5.71 us (2%)
    all_to_all x1, waiting for transfers between devices, local(): lax.all_to_all(jnp.stack([prefix_values] * lax.axis_size('seq')), 'seq',...  57.1 us
    all_gather x1, waiting for transfers between devices, local(): keys_piece = lax.all_gather(prefix_keys, 'seq', axis=1, tiled=True)  56.3 us
    all_gather x1, waiting for transfers between devices, local(): lax.all_gather(combined, 'seq', axis=0, tiled=True)  53.1 us
    dot_general x8, matrix products, inner(): jnp.einsum('bgqd,plgd->bgqpl', own_blocks, key_block, preferred_element_t...  28.8 us
    dot_general x8, matrix products, inner(): jnp.einsum('bgqpl,plgd->bgqd', weights.astype(jnp.bfloat16), value_block,...  28.7 us
    all_to_all x1, starting transfers between devices, local(): lax.all_to_all(jnp.stack([prefix_values] * lax.axis_size('seq')), 'seq',...  13.3 us
    dot_general x1, matrix products, local(): jnp.dot(normed, lax.all_gather(combined, 'seq', axis=0, tiled=True), pref...  9.91 us
    ppermute x3, starting transfers between devices, from_behind(): return lax.ppermute(shard, axis, pairs)  9.67 us
  transfers between devices with their start and end apart: 6, of which 3 were waited for; matrix products, arithmetic and copies ran while one was open for 30% of the time, Pallas kernels for 0%

profile of v1, /device:TPU:1, one launch (start us, length us, event | category | flops | bytes accessed | tf_op | source)
XLA Modules:
  0.0 309.8 jit_solution(15663743792454619223)
XLA Ops:
  7.2 0.9 copy.127
  8.1 1.7 pad_maximum_fusion
  9.9 2.8 stack.2
  12.6 13.3 %all-to-all-start = ((bf16[64,2,64,1,128]{4,2,1,3,0:T(8,128)(2,1)}), bf16[64,2,64,1,128]{4,2,1,3,0:T(8,128)(2,1)}, u32[]{:S(2)}, u32[]{:S(2)}) async-start(bf16[64,2,64,1,128]{4,2,1,3,0:T(8,128)(2,1)} %stack.2), calls=%async_computation | async-start | bytes 4194304 | tf_op jit(solution)/shard_map/all_to_all | solution.py:106
  26.0 0.7 all-gather.3.cloned.1.call-update
  27.4 3.1 %gather_fusion = s32[512]{0:T(512)S(1)} fusion(s32[8192]{0:T(1024)S(1)} %convert_reduce_fusion, s32[1024]{0:T(1024)S(1)} %pad_clamp_fusion), kind=kCustom, calls=%fused_computation | custom fusion | bytes 6144 | tf_op jit(solution)/shard_map/gather | solution.py:152
  32.3 57.1 %all-to-all-done = bf16[64,2,64,1,128]{4,2,1,3,0:T(8,128)(2,1)} async-done(((bf16[64,2,64,1,128]{4,2,1,3,0:T(8,128)(2,1)}), bf16[64,2,64,1,128]{4,2,1,3,0:T(8,128)(2,1)}, u32[]{:S(2)}, u32[]{:S(2)}) %all-to-all-start) | async-done | bytes 2097184 | tf_op jit(solution)/shard_map/all_to_all | solution.py:106
  89.4 3.1 %copy.68 = bf16[64,2,64,1,128]{4,2,0,1,3:T(8,128)(2,1)} copy(bf16[64,2,64,1,128]{4,2,1,3,0:T(8,128)(2,1)} %all-to-all-done) | data formatting | bytes 4194304 | tf_op jit(solution)/shard_map/all_to_all | solution.py:106
  92.5 53.1 %all-gather.5.cloned.1.call-done = bf16[8192,1280]{1,0:T(8,128)(2,1)} async-done(((bf16[128,1280]{1,0:T(8,128)(2,1)}), bf16[8192,1280]{1,0:T(8,128)(2,1)}) %all-gather.5.cloned.1.call-update) | async-done | bytes 20971536 | tf_op jit(solution)/shard_map/all_gather | solution.py:83
  145.6 9.9 %fusion.29 = f32[128,1280]{1,0:T(8,128)S(1)} fusion(bf16[8192,1280]{1,0:T(8,128)(2,1)} %all-gather.5.cloned.1.call-done, bf16[128,8192]{1,0:T(8,128)(2,1)S(1)} %copy-done.1, f32[8192]{0:T(1024)S(1)} %convert_element_type.68, f32[128]{0:T(128)S(1)} %add_rsqrt_fusion), kind=kOutput, calls=%fused_computation.34 | convolution fusion | flops 2688548864 | bytes 23757312 | tf_op jit(solution)/shard_map/dot_general | solution.py:81
  155.9 2.5 collective-permute-start
  158.3 5.0 %collective-permute-start.1 = (bf16[128,256]{1,0:T(8,128)(2,1)S(1)}, bf16[128,256]{1,0:T(8,128)(2,1)}, u32[]{:S(2)}, u32[]{:S(2)}) collective-permute-start(bf16[128,256]{1,0:T(8,128)(2,1)S(1)} %pad_maximum_fusion.3), channel_id=1, source_target_pairs={{0,8},{4,12},{8,16},{12,20},{16,24},{20,28},{24,32},{28,36},{32,40... | collective-permute-start | bytes 196616 | tf_op jit(solution)/shard_map/ppermute | solution.py:14
  163.4 2.2 collective-permute-start.2
  166.5 56.3 %all-gather.3.cloned.1.call-done = bf16[2,4096,1,128]{3,1,0,2:T(8,128)(2,1)} async-done(((bf16[2,64,1,128]{3,1,0,2:T(8,128)(2,1)}), bf16[2,4096,1,128]{3,1,0,2:T(8,128)(2,1)}) %all-gather.3.cloned.1.call-update) | async-done | bytes 2097168 | tf_op jit(solution)/shard_map/all_gather | solution.py:104
  222.8 74.9 %while.15 = (s32[]{:T(128)}, f32[128,1,8]{0,2,1:T(8,128)S(1)}, f32[128,1,8]{0,2,1:T(8,128)S(1)}, f32[128,1,8,128]{0,3,2,1:T(8,128)S(1)}, s32[8]{0:T(128)S(1)}, /...) while((s32[]{:T(128)}, f32[128,1,8]{0,2,1:T(8,128)S(1)}, ...), condition=%wide.region_8.9_spmd.clone, body=%wide.region_5.8_spmd.clone.sunk | while | flops 548804864 | bytes 31262436 | solution.py:134
  224.0 3.6 %fusion.78 = (f32[128,8]{0,1:T(8,128)S(1)}, f32[2,512,128,8]{2,1,3,0:T(8,128)}) fusion(pred[128,2]{0,1:T(4,128)(4,1)S(1)} %compare_bitcast_fusion.2, bf16[128,1,8,128]{3,0,2,1:T(8,128)(2,1)S(1)} %get-tuple-element.254, bf16[2,4096,1,128]{3,1,0,2:T(8,128)(2,1)} %get-tuple-element.253, s32[]{:T(128)S(6)} %select_n.55), kind=kOutput, calls=%fused_computation.6.clone.1 | convolution fusion | flops 271580160 | bytes 4722948 | tf_op jit(solution)/shard_map/while/body/eval_jaxpr/bgqd,plgd->bgqpl/dot_general | solution.py:116
  227.6 3.6 %fusion.81 = f32[128,1,8,128]{0,3,2,1:T(8,128)S(1)} fusion(f32[2,512,128,8]{2,1,3,0:T(8,128)} %get-tuple-element.220, f32[128,8]{0,1:T(8,128)S(1)} %bitcast.213, pred[128,2]{0,1:T(4,128)(4,1)S(1)} %compare_bitcast_fusion.2, f32[128,1,8,128]{0,3,2,1:T(8,128)S(1)} %get-tuple-element.238, bf16[2,4096,1,128]{3,1,0,2:T(8,128)(2,1)} %get-tuple-element.255, ...), kind=kOutput, calls=%fused_computation.11.clone.1 | convolution fusion | flops 273022976 | bytes 5513477 | tf_op jit(solution)/shard_map/while/body/eval_jaxpr/bgqpl,plgd->bgqd/dot_general | solution.py:126
  231.2 0.8 fusion.80
  232.1 0.6 dynamic_slice.46
  233.4 3.6 %fusion.78 = (f32[128,8]{0,1:T(8,128)S(1)}, f32[2,512,128,8]{2,1,3,0:T(8,128)}) fusion(pred[128,2]{0,1:T(4,128)(4,1)S(1)} %compare_bitcast_fusion.2, bf16[128,1,8,128]{3,0,2,1:T(8,128)(2,1)S(1)} %get-tuple-element.254, bf16[2,4096,1,128]{3,1,0,2:T(8,128)(2,1)} %get-tuple-element.253, s32[]{:T(128)S(6)} %select_n.55), kind=kOutput, calls=%fused_computation.6.clone.1 | convolution fusion | flops 271580160 | bytes 4722948 | tf_op jit(solution)/shard_map/while/body/eval_jaxpr/bgqd,plgd->bgqpl/dot_general | solution.py:116
  237.0 3.6 %fusion.81 = f32[128,1,8,128]{0,3,2,1:T(8,128)S(1)} fusion(f32[2,512,128,8]{2,1,3,0:T(8,128)} %get-tuple-element.220, f32[128,8]{0,1:T(8,128)S(1)} %bitcast.213, pred[128,2]{0,1:T(4,128)(4,1)S(1)} %compare_bitcast_fusion.2, f32[128,1,8,128]{0,3,2,1:T(8,128)S(1)} %get-tuple-element.238, bf16[2,4096,1,128]{3,1,0,2:T(8,128)(2,1)} %get-tuple-element.255, ...), kind=kOutput, calls=%fused_computation.11.clone.1 | convolution fusion | flops 273022976 | bytes 5513477 | tf_op jit(solution)/shard_map/while/body/eval_jaxpr/bgqpl,plgd->bgqd/dot_general | solution.py:126
  240.6 0.8 fusion.80
  241.5 0.6 dynamic_slice.46
  242.7 3.6 %fusion.78 = (f32[128,8]{0,1:T(8,128)S(1)}, f32[2,512,128,8]{2,1,3,0:T(8,128)}) fusion(pred[128,2]{0,1:T(4,128)(4,1)S(1)} %compare_bitcast_fusion.2, bf16[128,1,8,128]{3,0,2,1:T(8,128)(2,1)S(1)} %get-tuple-element.254, bf16[2,4096,1,128]{3,1,0,2:T(8,128)(2,1)} %get-tuple-element.253, s32[]{:T(128)S(6)} %select_n.55), kind=kOutput, calls=%fused_computation.6.clone.1 | convolution fusion | flops 271580160 | bytes 4722948 | tf_op jit(solution)/shard_map/while/body/eval_jaxpr/bgqd,plgd->bgqpl/dot_general | solution.py:116
  246.3 3.6 %fusion.81 = f32[128,1,8,128]{0,3,2,1:T(8,128)S(1)} fusion(f32[2,512,128,8]{2,1,3,0:T(8,128)} %get-tuple-element.220, f32[128,8]{0,1:T(8,128)S(1)} %bitcast.213, pred[128,2]{0,1:T(4,128)(4,1)S(1)} %compare_bitcast_fusion.2, f32[128,1,8,128]{0,3,2,1:T(8,128)S(1)} %get-tuple-element.238, bf16[2,4096,1,128]{3,1,0,2:T(8,128)(2,1)} %get-tuple-element.255, ...), kind=kOutput, calls=%fused_computation.11.clone.1 | convolution fusion | flops 273022976 | bytes 5513477 | tf_op jit(solution)/shard_map/while/body/eval_jaxpr/bgqpl,plgd->bgqd/dot_general | solution.py:126
  250.0 0.8 fusion.80
  250.8 0.6 dynamic_slice.46
  252.1 3.6 %fusion.78 = (f32[128,8]{0,1:T(8,128)S(1)}, f32[2,512,128,8]{2,1,3,0:T(8,128)}) fusion(pred[128,2]{0,1:T(4,128)(4,1)S(1)} %compare_bitcast_fusion.2, bf16[128,1,8,128]{3,0,2,1:T(8,128)(2,1)S(1)} %get-tuple-element.254, bf16[2,4096,1,128]{3,1,0,2:T(8,128)(2,1)} %get-tuple-element.253, s32[]{:T(128)S(6)} %select_n.55), kind=kOutput, calls=%fused_computation.6.clone.1 | convolution fusion | flops 271580160 | bytes 4722948 | tf_op jit(solution)/shard_map/while/body/eval_jaxpr/bgqd,plgd->bgqpl/dot_general | solution.py:116
  255.7 3.6 %fusion.81 = f32[128,1,8,128]{0,3,2,1:T(8,128)S(1)} fusion(f32[2,512,128,8]{2,1,3,0:T(8,128)} %get-tuple-element.220, f32[128,8]{0,1:T(8,128)S(1)} %bitcast.213, pred[128,2]{0,1:T(4,128)(4,1)S(1)} %compare_bitcast_fusion.2, f32[128,1,8,128]{0,3,2,1:T(8,128)S(1)} %get-tuple-element.238, bf16[2,4096,1,128]{3,1,0,2:T(8,128)(2,1)} %get-tuple-element.255, ...), kind=kOutput, calls=%fused_computation.11.clone.1 | convolution fusion | flops 273022976 | bytes 5513477 | tf_op jit(solution)/shard_map/while/body/eval_jaxpr/bgqpl,plgd->bgqd/dot_general | solution.py:126
  259.3 0.8 fusion.80
  260.2 0.6 dynamic_slice.46
  261.5 3.6 %fusion.78 = (f32[128,8]{0,1:T(8,128)S(1)}, f32[2,512,128,8]{2,1,3,0:T(8,128)}) fusion(pred[128,2]{0,1:T(4,128)(4,1)S(1)} %compare_bitcast_fusion.2, bf16[128,1,8,128]{3,0,2,1:T(8,128)(2,1)S(1)} %get-tuple-element.254, bf16[2,4096,1,128]{3,1,0,2:T(8,128)(2,1)} %get-tuple-element.253, s32[]{:T(128)S(6)} %select_n.55), kind=kOutput, calls=%fused_computation.6.clone.1 | convolution fusion | flops 271580160 | bytes 4722948 | tf_op jit(solution)/shard_map/while/body/eval_jaxpr/bgqd,plgd->bgqpl/dot_general | solution.py:116
  265.1 3.6 %fusion.81 = f32[128,1,8,128]{0,3,2,1:T(8,128)S(1)} fusion(f32[2,512,128,8]{2,1,3,0:T(8,128)} %get-tuple-element.220, f32[128,8]{0,1:T(8,128)S(1)} %bitcast.213, pred[128,2]{0,1:T(4,128)(4,1)S(1)} %compare_bitcast_fusion.2, f32[128,1,8,128]{0,3,2,1:T(8,128)S(1)} %get-tuple-element.238, bf16[2,4096,1,128]{3,1,0,2:T(8,128)(2,1)} %get-tuple-element.255, ...), kind=kOutput, calls=%fused_computation.11.clone.1 | convolution fusion | flops 273022976 | bytes 5513477 | tf_op jit(solution)/shard_map/while/body/eval_jaxpr/bgqpl,plgd->bgqd/dot_general | solution.py:126
  268.7 0.8 fusion.80
  269.6 0.6 dynamic_slice.46
  270.8 3.6 %fusion.78 = (f32[128,8]{0,1:T(8,128)S(1)}, f32[2,512,128,8]{2,1,3,0:T(8,128)}) fusion(pred[128,2]{0,1:T(4,128)(4,1)S(1)} %compare_bitcast_fusion.2, bf16[128,1,8,128]{3,0,2,1:T(8,128)(2,1)S(1)} %get-tuple-element.254, bf16[2,4096,1,128]{3,1,0,2:T(8,128)(2,1)} %get-tuple-element.253, s32[]{:T(128)S(6)} %select_n.55), kind=kOutput, calls=%fused_computation.6.clone.1 | convolution fusion | flops 271580160 | bytes 4722948 | tf_op jit(solution)/shard_map/while/body/eval_jaxpr/bgqd,plgd->bgqpl/dot_general | solution.py:116
  274.4 3.6 %fusion.81 = f32[128,1,8,128]{0,3,2,1:T(8,128)S(1)} fusion(f32[2,512,128,8]{2,1,3,0:T(8,128)} %get-tuple-element.220, f32[128,8]{0,1:T(8,128)S(1)} %bitcast.213, pred[128,2]{0,1:T(4,128)(4,1)S(1)} %compare_bitcast_fusion.2, f32[128,1,8,128]{0,3,2,1:T(8,128)S(1)} %get-tuple-element.238, bf16[2,4096,1,128]{3,1,0,2:T(8,128)(2,1)} %get-tuple-element.255, ...), kind=kOutput, calls=%fused_computation.11.clone.1 | convolution fusion | flops 273022976 | bytes 5513477 | tf_op jit(solution)/shard_map/while/body/eval_jaxpr/bgqpl,plgd->bgqd/dot_general | solution.py:126
  278.0 0.8 fusion.80
  278.9 0.6 dynamic_slice.46
  280.2 3.6 %fusion.78 = (f32[128,8]{0,1:T(8,128)S(1)}, f32[2,512,128,8]{2,1,3,0:T(8,128)}) fusion(pred[128,2]{0,1:T(4,128)(4,1)S(1)} %compare_bitcast_fusion.2, bf16[128,1,8,128]{3,0,2,1:T(8,128)(2,1)S(1)} %get-tuple-element.254, bf16[2,4096,1,128]{3,1,0,2:T(8,128)(2,1)} %get-tuple-element.253, s32[]{:T(128)S(6)} %select_n.55), kind=kOutput, calls=%fused_computation.6.clone.1 | convolution fusion | flops 271580160 | bytes 4722948 | tf_op jit(solution)/shard_map/while/body/eval_jaxpr/bgqd,plgd->bgqpl/dot_general | solution.py:116
  283.8 3.6 %fusion.81 = f32[128,1,8,128]{0,3,2,1:T(8,128)S(1)} fusion(f32[2,512,128,8]{2,1,3,0:T(8,128)} %get-tuple-element.220, f32[128,8]{0,1:T(8,128)S(1)} %bitcast.213, pred[128,2]{0,1:T(4,128)(4,1)S(1)} %compare_bitcast_fusion.2, f32[128,1,8,128]{0,3,2,1:T(8,128)S(1)} %get-tuple-element.238, bf16[2,4096,1,128]{3,1,0,2:T(8,128)(2,1)} %get-tuple-element.255, ...), kind=kOutput, calls=%fused_computation.11.clone.1 | convolution fusion | flops 273022976 | bytes 5513477 | tf_op jit(solution)/shard_map/while/body/eval_jaxpr/bgqpl,plgd->bgqd/dot_general | solution.py:126
  287.4 0.8 fusion.80
  289.5 3.6 %fusion.78 = (f32[128,8]{0,1:T(8,128)S(1)}, f32[2,512,128,8]{2,1,3,0:T(8,128)}) fusion(pred[128,2]{0,1:T(4,128)(4,1)S(1)} %compare_bitcast_fusion.2, bf16[128,1,8,128]{3,0,2,1:T(8,128)(2,1)S(1)} %get-tuple-element.254, bf16[2,4096,1,128]{3,1,0,2:T(8,128)(2,1)} %get-tuple-element.253, s32[]{:T(128)S(6)} %select_n.55), kind=kOutput, calls=%fused_computation.6.clone.1 | convolution fusion | flops 271580160 | bytes 4722948 | tf_op jit(solution)/shard_map/while/body/eval_jaxpr/bgqd,plgd->bgqpl/dot_general | solution.py:116
  293.2 3.6 %fusion.81 = f32[128,1,8,128]{0,3,2,1:T(8,128)S(1)} fusion(f32[2,512,128,8]{2,1,3,0:T(8,128)} %get-tuple-element.220, f32[128,8]{0,1:T(8,128)S(1)} %bitcast.213, pred[128,2]{0,1:T(4,128)(4,1)S(1)} %compare_bitcast_fusion.2, f32[128,1,8,128]{0,3,2,1:T(8,128)S(1)} %get-tuple-element.238, bf16[2,4096,1,128]{3,1,0,2:T(8,128)(2,1)} %get-tuple-element.255, ...), kind=kOutput, calls=%fused_computation.11.clone.1 | convolution fusion | flops 273022976 | bytes 5513477 | tf_op jit(solution)/shard_map/while/body/eval_jaxpr/bgqpl,plgd->bgqd/dot_general | solution.py:126
  296.8 0.8 fusion.80
  297.6 0.6 slice_bitcast_fusion.6
  298.5 0.9 maximum_maximum_fusion
  301.9 1.0 fusion.39
  (120 shorter events, 7.6 us)
Async XLA Ops:
  7.2 19.6 %copy-start.6 = (s32[32]{0:T(128)S(1)}, s32[32]{0:T(128)}, u32[]{:S(2)}) copy-start(s32[32]{0:T(128)} %param.20) | copy-start | bytes 388
  7.2 19.8 %copy-start.3 = (bf16[8192]{0:T(1024)(128)(2,1)S(1)}, bf16[8192]{0:T(1024)(128)(2,1)}, u32[]{:S(2)}) copy-start(bf16[8192]{0:T(1024)(128)(2,1)} %param.13) | copy-start | bytes 49156
  7.2 138.5 %all-gather.5.cloned.1.call-start = ((), (), s32[]{:S(2)}) async-start(), calls=%async_computation.2 | async-start | bytes 21299200 | tf_op jit(solution)/shard_map/all_gather | solution.py:83
  9.8 20.7 %copy-start.4 = (bf16[1024]{0:T(1024)(128)(2,1)S(1)}, bf16[1024]{0:T(1024)(128)(2,1)}, u32[]{:S(2)}) copy-start(bf16[1024]{0:T(1024)(128)(2,1)} %param.15) | copy-start | bytes 6148
  9.8 20.7 %copy-start.5 = (s32[32]{0:T(128)S(1)}, s32[32]{0:T(128)}, u32[]{:S(2)}) copy-start(s32[32]{0:T(128)} %param.21) | copy-start | bytes 388
  9.9 21.2 %copy-start.1 = (bf16[128,8192]{1,0:T(8,128)(2,1)S(1)}, bf16[128,8192]{1,0:T(8,128)(2,1)}, u32[]{:S(2)}) copy-start(bf16[128,8192]{1,0:T(8,128)(2,1)} %param.12) | copy-start | bytes 6291460
  12.6 19.0 %copy-start.7 = (bf16[2,128]{1,0:T(2,128)(2,1)S(1)}, bf16[2,128]{1,0:T(2,128)(2,1)}, u32[]{:S(2)}) copy-start(bf16[2,128]{1,0:T(2,128)(2,1)} %param.17) | copy-start | bytes 1540
  12.6 76.7 %all-to-all-start = ((bf16[64,2,64,1,128]{4,2,1,3,0:T(8,128)(2,1)}), bf16[64,2,64,1,128]{4,2,1,3,0:T(8,128)(2,1)}, u32[]{:S(2)}, u32[]{:S(2)}) async-start(bf16[64,2,64,1,128]{4,2,1,3,0:T(8,128)(2,1)} %stack.2), calls=%async_computation | async-start | bytes 4194304 | tf_op jit(solution)/shard_map/all_to_all | solution.py:106
  25.9 196.8 %all-gather.3.cloned.1.call-start = ((), (), s32[]{:S(2)}) async-start(), calls=%async_computation.1 | async-start | bytes 2129920 | tf_op jit(solution)/shard_map/all_gather | solution.py:104
  155.8 142.7 %copy-start.2 = (bf16[128,128]{1,0:T(8,128)(2,1)}, bf16[128,128]{1,0:T(8,128)(2,1)S(1)}, u32[]{:S(2)}) copy-start(bf16[128,128]{1,0:T(8,128)(2,1)S(1)} %get-tuple-element.148) | copy-start | bytes 98308
  155.9 142.6 %collective-permute-start = (bf16[128,256]{1,0:T(8,128)(2,1)S(1)}, bf16[128,256]{1,0:T(8,128)(2,1)S(1)}, u32[]{:S(2)}, u32[]{:S(2)}) collective-permute-start(bf16[128,256]{1,0:T(8,128)(2,1)S(1)} %pad_maximum_fusion.3), channel_id=1, source_target_pairs={{0,12},{4,16},{8,20},{12,24},{16,28},{20,32},{24,36},{28,40},{32,4... | collective-permute-start | bytes 196616 | tf_op jit(solution)/shard_map/ppermute | solution.py:14
  158.3 140.1 %collective-permute-start.1 = (bf16[128,256]{1,0:T(8,128)(2,1)S(1)}, bf16[128,256]{1,0:T(8,128)(2,1)}, u32[]{:S(2)}, u32[]{:S(2)}) collective-permute-start(bf16[128,256]{1,0:T(8,128)(2,1)S(1)} %pad_maximum_fusion.3), channel_id=1, source_target_pairs={{0,8},{4,12},{8,16},{12,20},{16,24},{20,28},{24,32},{28,36},{32,40... | collective-permute-start | bytes 196616 | tf_op jit(solution)/shard_map/ppermute | solution.py:14
  163.4 135.1 %collective-permute-start.2 = (bf16[128,256]{1,0:T(8,128)(2,1)S(1)}, bf16[128,256]{1,0:T(8,128)(2,1)}, u32[]{:S(2)}, u32[]{:S(2)}) collective-permute-start(bf16[128,256]{1,0:T(8,128)(2,1)S(1)} %pad_maximum_fusion.3), channel_id=1, source_target_pairs={{0,4},{4,8},{8,12},{12,16},{16,20},{20,24},{24,28},{28,32},{32,36}... | collective-permute-start | bytes 196616 | tf_op jit(solution)/shard_map/ppermute | solution.py:14
  227.6 3.6 %copy-start = (f32[2,512,128,8]{2,1,3,0:T(8,128)S(1)}, f32[2,512,128,8]{2,1,3,0:T(8,128)}, u32[]{:S(2)}) copy-start(f32[2,512,128,8]{2,1,3,0:T(8,128)} %get-tuple-element.220) | copy-start | bytes 12582916 | tf_op jit(solution)/shard_map/while
  237.0 3.6 %copy-start = (f32[2,512,128,8]{2,1,3,0:T(8,128)S(1)}, f32[2,512,128,8]{2,1,3,0:T(8,128)}, u32[]{:S(2)}) copy-start(f32[2,512,128,8]{2,1,3,0:T(8,128)} %get-tuple-element.220) | copy-start | bytes 12582916 | tf_op jit(solution)/shard_map/while
  246.3 3.6 %copy-start = (f32[2,512,128,8]{2,1,3,0:T(8,128)S(1)}, f32[2,512,128,8]{2,1,3,0:T(8,128)}, u32[]{:S(2)}) copy-start(f32[2,512,128,8]{2,1,3,0:T(8,128)} %get-tuple-element.220) | copy-start | bytes 12582916 | tf_op jit(solution)/shard_map/while
  255.7 3.6 %copy-start = (f32[2,512,128,8]{2,1,3,0:T(8,128)S(1)}, f32[2,512,128,8]{2,1,3,0:T(8,128)}, u32[]{:S(2)}) copy-start(f32[2,512,128,8]{2,1,3,0:T(8,128)} %get-tuple-element.220) | copy-start | bytes 12582916 | tf_op jit(solution)/shard_map/while
  265.1 3.6 %copy-start = (f32[2,512,128,8]{2,1,3,0:T(8,128)S(1)}, f32[2,512,128,8]{2,1,3,0:T(8,128)}, u32[]{:S(2)}) copy-start(f32[2,512,128,8]{2,1,3,0:T(8,128)} %get-tuple-element.220) | copy-start | bytes 12582916 | tf_op jit(solution)/shard_map/while
  274.4 3.6 %copy-start = (f32[2,512,128,8]{2,1,3,0:T(8,128)S(1)}, f32[2,512,128,8]{2,1,3,0:T(8,128)}, u32[]{:S(2)}) copy-start(f32[2,512,128,8]{2,1,3,0:T(8,128)} %get-tuple-element.220) | copy-start | bytes 12582916 | tf_op jit(solution)/shard_map/while
  283.8 3.6 %copy-start = (f32[2,512,128,8]{2,1,3,0:T(8,128)S(1)}, f32[2,512,128,8]{2,1,3,0:T(8,128)}, u32[]{:S(2)}) copy-start(f32[2,512,128,8]{2,1,3,0:T(8,128)} %get-tuple-element.220) | copy-start | bytes 12582916 | tf_op jit(solution)/shard_map/while
  293.1 3.6 %copy-start = (f32[2,512,128,8]{2,1,3,0:T(8,128)S(1)}, f32[2,512,128,8]{2,1,3,0:T(8,128)}, u32[]{:S(2)}) copy-start(f32[2,512,128,8]{2,1,3,0:T(8,128)} %get-tuple-element.220) | copy-start | bytes 12582916 | tf_op jit(solution)/shard_map/while
Sparse Core Ops, SparseCore 0:
  10.7 134.8 all-gather.4
  148.4 74.2 all-gather.2
